TPU v7x, 32 devices: a whole 2x2x4 slice. The times are simulated.
32 devices in a mesh: seq: 8 (over z, x), tensor: 4 (over y, core).
Axes of the slice: x: 2, y: 2, z: 4, core: 2. Of those that a mesh axis runs over, the one named last changes fastest.
Arguments:
- hidden: bfloat16 [4096, 1280], P(('seq', 'tensor')), may hold values from -6 to 6
- segment_ids: int32 [4096], P('seq'), may hold values from 0 to 3, never falling along the last dimension, each value on 1 to 2048 neighbouring positions
- page_slot: int32 [32], replicated, may hold values from 0 to 31, each once
- in_proj: bfloat16 [1280, 16, 192], P(None, 'tensor'), may hold values from -6 to 6
- out_proj: bfloat16 [1024, 1280], P('tensor'), may hold values from -0.1875 to 0.1875
- up_proj: bfloat16 [1280, 2, 5120], P(None, None, 'tensor'), may hold values from -6 to 6
- down_proj: bfloat16 [5120, 1280], P('tensor'), may hold values from -0.078125 to 0.078125
- score_scale: float32 [16, 64], P('tensor'), may hold values from 0.5 to 2
- mlp_scale: float32 [2, 5120], P(None, 'tensor'), may hold values from 0.5 to 2
- step_rates: float32 [2, 1280], replicated, may hold values from 0.05 to 0.5
Outputs:
- out_state: bfloat16 [4096, 1280], P(('seq', 'tensor'))
- page_cache: bfloat16 [32, 128, 2048], P('seq', None, 'tensor')
Inputs may be any that keep to these rules, and one draw needn't show every extreme that they name: `segment_ids`: never falling along the tokens; each prompt has 1 to 2048 tokens, one exactly 2048. `page_slot`: each slot named by exactly one page.
All inputs are finite; a program needn't handle non-finite values.
Results may differ from a plain program's by a relative error of at most 0.012.
Values may be sent and summed in bfloat16 or wider, within the bound.
No kernel may reach another device: no remote copies, remote signals or barrier semaphores. Data moves between devices by JAX's collectives and lax.ppermute only.
A program may use at most 128 MiB of HBM per device.

v0:
```python
import functools
import math

import jax
import jax.numpy as jnp
from jax import lax
from jax.experimental import pallas as pl
from jax.experimental.pallas import tpu as pltpu
from jax.sharding import PartitionSpec as P

PAGE = 128


EPSILON = 1e-06
NEG_LARGE = -1e30


def unit_rows(matrix):
    return matrix * lax.rsqrt(jnp.sum(matrix * matrix, axis=-1, keepdims=True) + EPSILON)


def gather_rows(part, axis):
    count = lax.axis_size(axis)
    index = lax.axis_index(axis)
    parts = [part]
    for shift in range(1, count):
        pairs = [(j, (j + shift) % count) for j in range(count)]
        parts.append(lax.ppermute(part, axis, pairs))
    stacked = jnp.stack(parts)
    order = (index - jnp.arange(count)) % count
    return jnp.zeros_like(stacked).at[order].set(stacked).reshape(-1, *part.shape[1:])


def scatter_sum(whole, axis):
    count = lax.axis_size(axis)
    index = lax.axis_index(axis)
    blocks = whole.reshape(count, whole.shape[0] // count, *whole.shape[1:])
    total = lax.dynamic_index_in_dim(blocks, index, 0, keepdims=False).astype(jnp.float32)
    for shift in range(1, count):
        pairs = [(j, (j + shift) % count) for j in range(count)]
        send = lax.dynamic_index_in_dim(blocks, (index + shift) % count, 0, keepdims=False)
        total = total + lax.ppermute(send, axis, pairs).astype(jnp.float32)
    return total


Q_TILE = 256
K_TILE = 256


def attend_kernel(
    bounds_ref, proj_ref, kv_ref, scale_ref, qseg_ref, kseg_ref, out_ref, *, factor, half
):
    rows = qseg_ref.shape[0]
    heads = scale_ref.shape[0]
    lanes = 2 * half
    shard_blocks = (kv_ref.shape[1] - kv_ref.shape[1] % K_TILE) // K_TILE
    tiles = rows // Q_TILE
    first = bounds_ref[2 * tiles]
    key_lane = lax.broadcasted_iota(jnp.int32, (K_TILE, lanes), 1)
    for head in range(heads):
        scale = scale_ref[head]
        for tile in range(tiles):
            q_raw = proj_ref[tile * Q_TILE : (tile + 1) * Q_TILE, head * 2 * lanes : head * 2 * lanes + lanes]
            q_tile = (
                q_raw * lax.rsqrt(jnp.sum(q_raw * q_raw, axis=1, keepdims=True) + EPSILON) * scale
            ).astype(jnp.bfloat16)
            q_seg = qseg_ref[tile * Q_TILE : (tile + 1) * Q_TILE, :]
            q_pos = first + tile * Q_TILE + lax.broadcasted_iota(jnp.int32, (Q_TILE, K_TILE), 0)

            def step(block, carry, q_tile=q_tile, q_seg=q_seg, q_pos=q_pos, head=head, scale=scale):
                top, total, acc = carry
                shard = block // shard_blocks
                row_at = pl.multiple_of((block % shard_blocks) * K_TILE, K_TILE)
                key_at = pl.multiple_of(block * K_TILE, K_TILE)
                kv_blk = kv_ref[shard, pl.ds(row_at, K_TILE), head * lanes : (head + 1) * lanes]
                kv_f = kv_blk.astype(jnp.float32)
                k_sq = jnp.where(key_lane < half, kv_f * kv_f, 0.0)
                k_unit = (
                    kv_f * lax.rsqrt(jnp.sum(k_sq, axis=1, keepdims=True) + EPSILON) * scale
                ).astype(jnp.bfloat16)
                k_seg = kseg_ref[:, pl.ds(key_at, K_TILE)]
                scores = factor * lax.dot_general(
                    q_tile, k_unit, (((1,), (1,)), ((), ())), preferred_element_type=jnp.float32
                )
                k_pos = key_at + lax.broadcasted_iota(jnp.int32, (Q_TILE, K_TILE), 1)
                allowed = (q_seg == k_seg) & (k_pos <= q_pos)
                scores = jnp.where(allowed, scores, NEG_LARGE)
                new_top = jnp.maximum(top, jnp.max(scores, axis=1, keepdims=True))
                weights = jnp.where(allowed, jnp.exp(scores - new_top), 0.0)
                rescale = jnp.exp(top - new_top)
                new_total = total * rescale + jnp.sum(weights, axis=1, keepdims=True)
                update = jnp.dot(
                    weights.astype(jnp.bfloat16), kv_blk, preferred_element_type=jnp.float32
                )
                return (new_top, new_total, acc * rescale + update)

            start = (
                jnp.full((Q_TILE, 1), NEG_LARGE, jnp.float32),
                jnp.zeros((Q_TILE, 1), jnp.float32),
                jnp.zeros((Q_TILE, lanes), jnp.float32),
            )
            top, total, acc = lax.fori_loop(
                bounds_ref[tile], bounds_ref[tiles + tile] + 1, step, start
            )
            out_ref[tile * Q_TILE : (tile + 1) * Q_TILE, head * lanes : (head + 1) * lanes] = (
                acc / total
            ).astype(out_ref.dtype)


def flash_attend(bounds, proj, gathered, scale_pad, query_segs, key_segs, factor, half):
    rows = query_segs.shape[0]
    heads, _, lanes = scale_pad.shape
    keys = key_segs.shape[1]
    vmem = pl.BlockSpec(memory_space=pltpu.VMEM)
    return pl.pallas_call(
        functools.partial(attend_kernel, factor=factor, half=half),
        out_shape=jax.ShapeDtypeStruct((rows, heads * lanes), jnp.bfloat16),
        in_specs=[pl.BlockSpec(memory_space=pltpu.SMEM)] + [vmem] * 5,
        out_specs=vmem,
        cost_estimate=pl.CostEstimate(
            flops=4 * heads * rows * keys * lanes,
            transcendentals=heads * rows * keys,
            bytes_accessed=heads * keys * lanes * 2,
        ),
    )(bounds, proj, gathered, scale_pad, query_segs, key_segs)


def body(
    hidden,
    segment_ids,
    page_slot,
    in_proj,
    out_proj,
    up_proj,
    down_proj,
    score_scale,
    mlp_scale,
    step_rates,
):
    seq_count = lax.axis_size("seq")
    seq_index = lax.axis_index("seq")
    local_tokens = segment_ids.shape[0]
    heads_dev, head_dim = score_scale.shape
    model_width = hidden.shape[1]
    hidden_dev = down_proj.shape[0]
    pages_dev = local_tokens // PAGE
    channels = heads_dev * 2 * head_dim
    state_own = unit_rows(hidden.astype(jnp.float32)).astype(jnp.bfloat16)
    gathered_state = gather_rows(state_own, "tensor")
    lanes = 2 * head_dim
    weight_pad = jnp.concatenate(
        [
            in_proj[:, :, :head_dim],
            jnp.zeros((model_width, heads_dev, head_dim), in_proj.dtype),
            in_proj[:, :, head_dim:],
        ],
        axis=2,
    ).reshape(model_width, heads_dev * 2 * lanes)
    projected = jnp.dot(gathered_state, weight_pad, preferred_element_type=jnp.float32)
    key_value = jnp.concatenate(
        [projected[:, (2 * h + 1) * lanes : (2 * h + 2) * lanes] for h in range(heads_dev)],
        axis=1,
    ).astype(jnp.bfloat16)
    first_token = seq_index * local_tokens
    seg_rows = -(-local_tokens // channels)
    seg_flat = jnp.pad(segment_ids, (0, seg_rows * channels - local_tokens))
    kv_ext = jnp.concatenate(
        [key_value, seg_flat.astype(jnp.bfloat16).reshape(seg_rows, channels)], axis=0
    )
    gathered = lax.all_gather(kv_ext, "seq", axis=0, tiled=False)
    seg_piece = (
        gathered[:, local_tokens:].reshape(seq_count, seg_rows * channels)[:, :local_tokens]
        .reshape(-1)
        .astype(jnp.int32)
    )
    piece_rows = seq_count * local_tokens
    scale_pad = jnp.pad(score_scale, ((0, 0), (0, lanes - head_dim))).reshape(heads_dev, 1, lanes)
    tiles = local_tokens // Q_TILE
    tile_first = first_token + Q_TILE * jnp.arange(tiles, dtype=jnp.int32)
    tile_seg = segment_ids.reshape(tiles, Q_TILE)[:, 0]
    block_last_seg = seg_piece.reshape(piece_rows // K_TILE, K_TILE)[:, -1]
    block_lo = jnp.sum(
        (block_last_seg[None, :] < tile_seg[:, None]).astype(jnp.int32), axis=1
    )
    block_hi = (tile_first + Q_TILE - 1) // K_TILE
    bounds = jnp.concatenate([block_lo, block_hi, first_token[None]]).astype(jnp.int32)
    heads_pad = flash_attend(
        bounds,
        projected,
        gathered,
        scale_pad,
        segment_ids.reshape(local_tokens, 1),
        seg_piece.reshape(1, piece_rows),
        math.sqrt(head_dim),
        head_dim,
    )
    out_pad = jnp.pad(
        out_proj.reshape(heads_dev, head_dim, model_width), ((0, 0), (head_dim, 0), (0, 0))
    ).reshape(heads_dev * lanes, model_width)
    slots_dev = page_slot.shape[0] // seq_count
    my_slots = seq_index * slots_dev + jnp.arange(slots_dev, dtype=jnp.int32)
    page_ids = jnp.arange(page_slot.shape[0], dtype=jnp.int32)
    source_page = jnp.sum(
        jnp.where(page_slot[None, :] == my_slots[:, None], page_ids[None, :], 0), axis=1
    )
    page_cache = jnp.stack(
        [
            lax.dynamic_slice(
                gathered,
                (source_page[j] // pages_dev, (source_page[j] % pages_dev) * PAGE, 0),
                (1, PAGE, channels),
            )[0]
            for j in range(slots_dev)
        ]
    )
    chosen = heads_pad
    attn_own = scatter_sum(
        jnp.dot(chosen, out_pad, preferred_element_type=jnp.float32).astype(jnp.bfloat16),
        "tensor",
    )
    state_f = state_own.astype(jnp.float32)
    middle = unit_rows(state_f + step_rates[0] * (unit_rows(attn_own) - state_f))
    mid_rows = gather_rows(middle.astype(jnp.bfloat16), "tensor")
    both = jnp.einsum("td,dkf->tkf", mid_rows, up_proj, preferred_element_type=jnp.float32)
    act = (
        both[:, 0] * mlp_scale[0] * jax.nn.silu(both[:, 1] * mlp_scale[1] * math.sqrt(model_width))
    ).astype(jnp.bfloat16)
    chosen = act
    mlp_own = scatter_sum(
        jnp.dot(chosen, down_proj, preferred_element_type=jnp.float32).astype(jnp.bfloat16),
        "tensor",
    )
    final = unit_rows(middle + step_rates[1] * (unit_rows(mlp_own) - middle))
    out_state = (math.sqrt(model_width) * final).astype(jnp.bfloat16)
    return (out_state, page_cache)


def solution(mesh):
    return jax.shard_map(
        body,
        mesh=mesh,
        in_specs=(
            P(("seq", "tensor"), None),
            P("seq"),
            P(),
            P(None, "tensor", None),
            P("tensor", None),
            P(None, None, "tensor"),
            P("tensor", None),
            P("tensor", None),
            P(None, "tensor"),
            P(),
        ),
        out_specs=(P(("seq", "tensor"), None), P("seq", None, "tensor")),
        check_vma=False,
    )
```

profile of v0, /device:TPU:26, one launch (start us, length us, event | category | flops | bytes accessed | tf_op | source)
XLA Modules:
  0.0 237.4 jit_solution(15068038338162949519)
XLA Ops:
  7.2 0.0 all-gather.4.cloned.1.call-start
  7.2 1.3 fusion.8
  8.5 1.8 fusion.9
  10.3 1.6 collective-permute-start.1
  11.9 1.4 collective-permute-start.2
  13.3 2.5 %slice.68 = bf16[1280,4,128]{0,2,1:T(8,128)(2,1)} slice(bf16[1280,4,192]{0,2,1:T(8,128)(2,1)} %param.13), slice={[0:1280], [0:4], [64:192]} | slice | bytes 2621440 | tf_op jit(solution)/shard_map/slice | solution.py:155
  15.8 2.0 slice.67
  17.8 0.1 pad.27.clone
  17.9 3.5 %pad_maximum_fusion = bf16[1280,4,256]{0,2,1:T(8,128)(2,1)} fusion(bf16[1280,4,128]{0,2,1:T(8,128)(2,1)} %slice.68, bf16[1280,4,64]{0,2,1:T(8,128)(2,1)} %slice.67, bf16[256]{0:T(256)(128)(2,1)S(1)} %pad.27.clone), kind=kLoop, calls=%fused_computation.13 | loop fusion | flops 7864320 | bytes 4588032 | tf_op jit(solution)/shard_map/concatenate | solution.py:151
  21.5 0.1 fusion.31
  21.6 5.1 %collective-permute-done.2 = bf16[128,1280]{1,0:T(8,128)(2,1)} collective-permute-done((bf16[128,1280]{1,0:T(8,128)(2,1)}, bf16[128,1280]{1,0:T(8,128)(2,1)}, u32[]{:S(2)}, u32[]{:S(2)}) %collective-permute-start.2) | collective-permute-done | bytes 327712 | tf_op jit(solution)/shard_map/ppermute | solution.py:28
  26.7 2.4 %pad_maximum_fusion.1 = bf16[4,128,1280]{2,1,0:T(8,128)(2,1)} fusion(bf16[1,128,1280]{2,1,0:T(8,128)(2,1)} %bitcast.4, bf16[1,128,1280]{2,1,0:T(8,128)(2,1)} %bitcast.3, bf16[1,128,1280]{2,1,0:T(8,128)(2,1)} %bitcast.2, bf16[1,128,1280]{2,1,0:T(8,128)(2,1)S(1)} %fusion.31), kind=kLoop, calls=%fused_computation.14 | loop fusion | flops 1966080 | bytes 2621440 | tf_op jit(solution)/shard_map/stack | solution.py:29
  29.1 1.2 broadcast.137.clone
  30.3 3.4 %scatter_fusion = bf16[4,128,1280]{2,1,0:T(8,128)(2,1)} fusion(bf16[4,128,1280]{2,1,0:T(8,128)(2,1)} %broadcast.137.clone, s32[4]{0:T(128)S(1)} %fusion.17, bf16[4,128,1280]{2,1,0:T(8,128)(2,1)} %pad_maximum_fusion.1), kind=kCustom, calls=%fused_computation | custom fusion | bytes 3932176 | tf_op jit(solution)/shard_map/scatter | solution.py:31
  33.7 5.0 %fusion.23 = (bf16[512,1024]{1,0:T(8,128)(2,1)S(1)}, f32[512,1024]{1,0:T(8,128)}) fusion(bf16[512,1280]{1,0:T(8,128)(2,1)} %bitcast.85, bf16[1280,1024]{0,1:T(8,128)(2,1)} %bitcast.86), kind=kOutput, calls=%fused_computation.80 | convolution fusion | flops 1342701568 | bytes 7077888 | tf_op jit(solution)/shard_map/dot_general | solution.py:159
  38.7 0.1 fusion.21
  38.8 0.9 maximum_bitcast_fusion
  39.7 0.0 all-gather.4.cloned.1.call-update
  39.8 0.9 copy.20.qseg_ref
  40.6 0.6 pad.8
  41.2 2.2 pad.9
  43.5 0.1 slice_reduce_fusion.4
  43.6 69.2 %all-gather.4.cloned.1.call-done.kv_ref = bf16[8,513,512]{2,1,0:T(8,128)(2,1)} async-done(((bf16[1,513,512]{2,1,0:T(8,128)(2,1)}), bf16[8,513,512]{2,1,0:T(8,128)(2,1)}) %all-gather.4.cloned.1.call-update) | async-done | bytes 4202512 | tf_op jit(solution)/shard_map/all_gather | solution.py:170
  112.8 0.9 fusion.20
  113.7 0.2 convert_reduce_fusion
  113.9 0.6 convert.17.kseg_ref
  114.5 0.2 fusion.15
  114.7 0.6 pad_add_fusion.bounds_ref
  115.3 41.6 %shard_map.113 = bf16[512,512]{1,0:T(8,128)(2,1)} custom-call(s32[5]{0:T(128)} %pad_add_fusion.bounds_ref, f32[512,1024]{1,0:T(8,128)} %get-tuple-element.31.proj_ref, bf16[8,513,512]{2,1,0:T(8,128)(2,1)} %all-gather.4.cloned.1.call-done.kv_ref, f32[4,1,128]{2,1,0:T(1,128)} %bitcast.100, s32[512,1]{1,0:T(8,128)} %copy.20.qseg_ref, s32[1,4096]{1,0:T(1,128)} %convert.17.kseg_ref), custom_call_target="tpu_custom_call" | custom-call | flops 4294967296 | bytes 4194304 | tf_op jit(solution)/shard_map/pallas_call | solution.py:115
  156.9 2.3 convolution_convert_fusion.1
  159.3 0.1 dynamic-slice_bitcast_fusion.5
  159.4 0.1 collective-permute-start.3
  159.5 1.5 collective-permute-start.4
  161.0 1.4 collective-permute-start.5
  162.4 0.2 select_reduce_fusion
  162.6 6.2 %collective-permute-done.3 = bf16[128,1280]{1,0:T(8,128)(2,1)S(1)} collective-permute-done((bf16[128,1280]{1,0:T(8,128)(2,1)S(1)}, bf16[128,1280]{1,0:T(8,128)(2,1)S(1)}, u32[]{:S(2)}, u32[]{:S(2)}) %collective-permute-start.3) | collective-permute-done | bytes 327712 | tf_op jit(solution)/shard_map/ppermute | solution.py:42
  168.8 1.2 collective-permute-done.4
  170.1 5.4 %collective-permute-done.5 = bf16[128,1280]{1,0:T(8,128)(2,1)S(1)} collective-permute-done((bf16[128,1280]{1,0:T(8,128)(2,1)S(1)}, bf16[128,1280]{1,0:T(8,128)(2,1)S(1)}, u32[]{:S(2)}, u32[]{:S(2)}) %collective-permute-start.5) | collective-permute-done | bytes 327712 | tf_op jit(solution)/shard_map/ppermute | solution.py:42
  175.5 0.3 multiply_reduce_fusion.3
  175.8 0.4 multiply_reduce_fusion.2
  176.2 0.1 multiply_convert_fusion.1
  176.3 0.9 collective-permute-start.6
  177.2 1.5 collective-permute-start.7
  178.7 0.1 fusion.30
  178.8 6.5 %collective-permute-done.6 = bf16[128,1280]{1,0:T(8,128)(2,1)S(1)} collective-permute-done((bf16[128,1280]{1,0:T(8,128)(2,1)S(1)}, bf16[128,1280]{1,0:T(8,128)(2,1)S(1)}, u32[]{:S(2)}, u32[]{:S(2)}) %collective-permute-start.6) | collective-permute-done | bytes 327712 | tf_op jit(solution)/shard_map/ppermute | solution.py:28
  185.3 2.6 %collective-permute-done.7 = bf16[128,1280]{1,0:T(8,128)(2,1)S(1)} collective-permute-done((bf16[128,1280]{1,0:T(8,128)(2,1)S(1)}, bf16[128,1280]{1,0:T(8,128)(2,1)S(1)}, u32[]{:S(2)}, u32[]{:S(2)}) %collective-permute-start.7) | collective-permute-done | bytes 327712 | tf_op jit(solution)/shard_map/ppermute | solution.py:28
  187.8 3.8 %collective-permute-done.8 = bf16[128,1280]{1,0:T(8,128)(2,1)S(1)} collective-permute-done((bf16[128,1280]{1,0:T(8,128)(2,1)S(1)}, bf16[128,1280]{1,0:T(8,128)(2,1)S(1)}, u32[]{:S(2)}, u32[]{:S(2)}) %collective-permute-start.8) | collective-permute-done | bytes 327712 | tf_op jit(solution)/shard_map/ppermute | solution.py:28
  191.7 1.3 pad_maximum_fusion.2
  192.9 1.1 broadcast.137
  194.1 3.4 %scatter_fusion.1 = bf16[4,128,1280]{2,1,0:T(8,128)(2,1)} fusion(bf16[4,128,1280]{2,1,0:T(8,128)(2,1)} %broadcast.137, s32[4]{0:T(128)S(1)} %fusion.17, bf16[4,128,1280]{2,1,0:T(8,128)(2,1)} %pad_maximum_fusion.2), kind=kCustom, calls=%fused_computation.1 | custom fusion | bytes 3932176 | tf_op jit(solution)/shard_map/scatter | solution.py:31
  197.5 6.7 %fusion = f32[512,2,1280]{2,0,1:T(8,128)S(1)} fusion(bf16[512,1280,1]{1,0,2:T(8,128)(2,1)} %bitcast.84, bf16[1280,2,1280]{2,1,0:T(2,128)(2,1)} %param.15), kind=kOutput, calls=%fused_computation.2 | convolution fusion | flops 3355443200 | bytes 13107200 | tf_op jit(solution)/shard_map/td,dkf->tkf/dot_general | solution.py:224
  204.2 2.5 %convolution_convert_fusion = bf16[512,1280]{1,0:T(8,128)(2,1)S(1)} fusion(bf16[1280,1280]{1,0:T(8,128)(2,1)S(1)} %copy-done, f32[512,2,1280]{2,0,1:T(8,128)S(1)} %fusion, f32[1280]{0:T(1024)S(1)} %get-tuple-element.5, f32[1280]{0:T(1024)S(1)} %get-tuple-element.4), kind=kOutput, calls=%fused_computation.4 | convolution fusion | flops 1684275200 | bytes 9840640 | tf_op jit(solution)/shard_map/dot_general | solution.py:230
  206.7 1.0 copy-done.5
  207.7 1.0 dynamic-slice_bitcast_fusion.2
  208.7 1.5 collective-permute-start.10
  210.2 1.6 collective-permute-start.11
  211.8 0.6 fusion.22
  222.4 1.4 constant_dynamic-slice_fusion.3
  223.7 0.9 pad_maximum_fusion.3
  224.6 0.9 collective-permute-done.11
  225.5 1.2 collective-permute-done.9
  226.6 1.4 multiply_reduce_fusion.1
  228.1 1.6 multiply_reduce_fusion
  229.7 0.9 multiply_convert_fusion
  (44 shorter events, 0.2 us)
Async XLA Ops:
  7.2 197.0 %copy-start = (bf16[1280,1280]{1,0:T(8,128)(2,1)S(1)}, bf16[1280,1280]{1,0:T(8,128)(2,1)}, u32[]{:S(2)}) copy-start(bf16[1280,1280]{1,0:T(8,128)(2,1)} %param.16) | copy-start | bytes 9830404
  7.2 105.6 %all-gather.4.cloned.1.call-start = ((), (), s32[]{:S(2)}) async-start(), calls=%async_computation | async-start | bytes 4792320 | tf_op jit(solution)/shard_map/all_gather | solution.py:170
  10.3 11.3 %collective-permute-start = (bf16[128,1280]{1,0:T(8,128)(2,1)}, bf16[128,1280]{1,0:T(8,128)(2,1)}, u32[]{:S(2)}, u32[]{:S(2)}) collective-permute-start(bf16[128,1280]{1,0:T(8,128)(2,1)} %fusion.9), channel_id=1, source_target_pairs={{0,1},{1,2},{2,3},{3,0},{4,5},{5,6},{6,7},{7,4},{8,9},{9,10},{10,1... | collective-permute-start | bytes 983048 | tf_op jit(solution)/shard_map/ppermute | solution.py:28
  10.3 11.3 %collective-permute-start.1 = (bf16[128,1280]{1,0:T(8,128)(2,1)}, bf16[128,1280]{1,0:T(8,128)(2,1)}, u32[]{:S(2)}, u32[]{:S(2)}) collective-permute-start(bf16[128,1280]{1,0:T(8,128)(2,1)} %fusion.9), channel_id=1, source_target_pairs={{0,2},{1,3},{2,0},{3,1},{4,6},{5,7},{6,4},{7,5},{8,10},{9,11},{10,... | collective-permute-start | bytes 983048 | tf_op jit(solution)/shard_map/ppermute | solution.py:28
  11.9 14.8 %collective-permute-start.2 = (bf16[128,1280]{1,0:T(8,128)(2,1)}, bf16[128,1280]{1,0:T(8,128)(2,1)}, u32[]{:S(2)}, u32[]{:S(2)}) collective-permute-start(bf16[128,1280]{1,0:T(8,128)(2,1)} %fusion.9), channel_id=1, source_target_pairs={{0,3},{1,0},{2,1},{3,2},{4,7},{5,4},{6,5},{7,6},{8,11},{9,8},{10,9... | collective-permute-start | bytes 983048 | tf_op jit(solution)/shard_map/ppermute | solution.py:28
  15.8 2.0 copy-start.7
  17.9 3.5 %copy-start.3 = (bf16[128,1280]{1,0:T(8,128)(2,1)S(1)}, bf16[128,1280]{1,0:T(8,128)(2,1)}, u32[]{:S(2)}) copy-start(bf16[128,1280]{1,0:T(8,128)(2,1)} %param.10) | copy-start | bytes 983044
  38.7 1.9 copy-start.10
  39.7 3.9 %copy-start.8 = (f32[2,1280]{1,0:T(2,128)S(1)}, f32[2,1280]{1,0:T(2,128)}, u32[]{:S(2)}) copy-start(f32[2,1280]{1,0:T(2,128)} %param.19) | copy-start | bytes 30724
  159.3 3.1 %copy-start.9 = (f32[2,1280]{1,0:T(2,128)S(1)}, f32[2,1280]{1,0:T(2,128)}, u32[]{:S(2)}) copy-start(f32[2,1280]{1,0:T(2,128)} %param.18) | copy-start | bytes 30724
  159.3 3.1 %copy-start.11 = (s32[32]{0:T(128)S(1)}, s32[32]{0:T(128)}, u32[]{:S(2)}) copy-start(s32[32]{0:T(128)} %param.12) | copy-start | bytes 388
  159.3 16.5 %copy-start.4 = (bf16[128,1280]{1,0:T(8,128)(2,1)S(1)}, bf16[128,1280]{1,0:T(8,128)(2,1)}, u32[]{:S(2)}) copy-start(bf16[128,1280]{1,0:T(8,128)(2,1)} %param.10) | copy-start | bytes 983044
  159.4 9.5 %collective-permute-start.3 = (bf16[128,1280]{1,0:T(8,128)(2,1)S(1)}, bf16[128,1280]{1,0:T(8,128)(2,1)S(1)}, u32[]{:S(2)}, u32[]{:S(2)}) collective-permute-start(bf16[128,1280]{1,0:T(8,128)(2,1)S(1)} %get-tuple-element.19), channel_id=1, source_target_pairs={{0,1},{1,2},{2,3},{3,0},{4,5},{5,6},{6,7},{7,4},{8,9},{9,10},{10,1... | collective-permute-start | bytes 983048 | tf_op jit(solution)/shard_map/ppermute | solution.py:42
  159.5 10.6 %collective-permute-start.4 = (bf16[128,1280]{1,0:T(8,128)(2,1)S(1)}, bf16[128,1280]{1,0:T(8,128)(2,1)S(1)}, u32[]{:S(2)}, u32[]{:S(2)}) collective-permute-start(bf16[128,1280]{1,0:T(8,128)(2,1)S(1)} %get-tuple-element.21), channel_id=1, source_target_pairs={{0,2},{1,3},{2,0},{3,1},{4,6},{5,7},{6,4},{7,5},{8,10},{9,11},{10,... | collective-permute-start | bytes 983048 | tf_op jit(solution)/shard_map/ppermute | solution.py:42
  161.0 14.5 %collective-permute-start.5 = (bf16[128,1280]{1,0:T(8,128)(2,1)S(1)}, bf16[128,1280]{1,0:T(8,128)(2,1)S(1)}, u32[]{:S(2)}, u32[]{:S(2)}) collective-permute-start(bf16[128,1280]{1,0:T(8,128)(2,1)S(1)} %get-tuple-element.20), channel_id=1, source_target_pairs={{0,3},{1,0},{2,1},{3,2},{4,7},{5,4},{6,5},{7,6},{8,11},{9,8},{10,9... | collective-permute-start | bytes 983048 | tf_op jit(solution)/shard_map/ppermute | solution.py:42
  176.2 2.5 %copy-start.1 = (f32[128,1280]{1,0:T(8,128)}, f32[128,1280]{1,0:T(8,128)S(1)}, u32[]{:S(2)}) copy-start(f32[128,1280]{1,0:T(8,128)S(1)} %get-tuple-element.9) | copy-start | bytes 1966084
  176.3 8.9 %collective-permute-start.6 = (bf16[128,1280]{1,0:T(8,128)(2,1)S(1)}, bf16[128,1280]{1,0:T(8,128)(2,1)S(1)}, u32[]{:S(2)}, u32[]{:S(2)}) collective-permute-start(bf16[128,1280]{1,0:T(8,128)(2,1)S(1)} %multiply_convert_fusion.1), channel_id=1, source_target_pairs={{0,1},{1,2},{2,3},{3,0},{4,5},{5,6},{6,7},{7,4},{8,9},{9,10},{10,1... | collective-permute-start | bytes 983048 | tf_op jit(solution)/shard_map/ppermute | solution.py:28
  177.2 10.6 %collective-permute-start.7 = (bf16[128,1280]{1,0:T(8,128)(2,1)S(1)}, bf16[128,1280]{1,0:T(8,128)(2,1)S(1)}, u32[]{:S(2)}, u32[]{:S(2)}) collective-permute-start(bf16[128,1280]{1,0:T(8,128)(2,1)S(1)} %multiply_convert_fusion.1), channel_id=1, source_target_pairs={{0,2},{1,3},{2,0},{3,1},{4,6},{5,7},{6,4},{7,5},{8,10},{9,11},{10,... | collective-permute-start | bytes 983048 | tf_op jit(solution)/shard_map/ppermute | solution.py:28
  178.7 13.0 %collective-permute-start.8 = (bf16[128,1280]{1,0:T(8,128)(2,1)S(1)}, bf16[128,1280]{1,0:T(8,128)(2,1)S(1)}, u32[]{:S(2)}, u32[]{:S(2)}) collective-permute-start(bf16[128,1280]{1,0:T(8,128)(2,1)S(1)} %multiply_convert_fusion.1), channel_id=1, source_target_pairs={{0,3},{1,0},{2,1},{3,2},{4,7},{5,4},{6,5},{7,6},{8,11},{9,8},{10,9... | collective-permute-start | bytes 983048 | tf_op jit(solution)/shard_map/ppermute | solution.py:28
  206.7 1.1 copy-start.5
  208.7 15.9 %collective-permute-start.10 = (bf16[128,1280]{1,0:T(8,128)(2,1)}, bf16[128,1280]{1,0:T(8,128)(2,1)}, u32[]{:S(2)}, u32[]{:S(2)}) collective-permute-start(bf16[128,1280]{1,0:T(8,128)(2,1)} %get-tuple-element.18), channel_id=1, source_target_pairs={{0,2},{1,3},{2,0},{3,1},{4,6},{5,7},{6,4},{7,5},{8,10},{9,11},{10,... | collective-permute-start | bytes 983048 | tf_op jit(solution)/shard_map/ppermute | solution.py:42
  210.2 15.3 %collective-permute-start.11 = (bf16[128,1280]{1,0:T(8,128)(2,1)}, bf16[128,1280]{1,0:T(8,128)(2,1)}, u32[]{:S(2)}, u32[]{:S(2)}) collective-permute-start(bf16[128,1280]{1,0:T(8,128)(2,1)} %get-tuple-element.17), channel_id=1, source_target_pairs={{0,3},{1,0},{2,1},{3,2},{4,7},{5,4},{6,5},{7,6},{8,11},{9,8},{10,9... | collective-permute-start | bytes 983048 | tf_op jit(solution)/shard_map/ppermute | solution.py:42
  211.8 14.8 %collective-permute-start.9 = (bf16[128,1280]{1,0:T(8,128)(2,1)}, bf16[128,1280]{1,0:T(8,128)(2,1)}, u32[]{:S(2)}, u32[]{:S(2)}) collective-permute-start(bf16[128,1280]{1,0:T(8,128)(2,1)} %get-tuple-element.16), channel_id=1, source_target_pairs={{0,1},{1,2},{2,3},{3,0},{4,5},{5,6},{6,7},{7,4},{8,9},{9,10},{10,1... | collective-permute-start | bytes 983048 | tf_op jit(solution)/shard_map/ppermute | solution.py:42
  222.4 4.3 %copy-start.6 = (bf16[512,1280]{1,0:T(8,128)(2,1)S(1)}, bf16[512,1280]{1,0:T(8,128)(2,1)}, u32[]{:S(2)}) copy-start(bf16[512,1280]{1,0:T(8,128)(2,1)} %copy-done.5) | copy-start | bytes 3932164
  223.7 4.4 %copy-start.2 = (f32[128,1280]{1,0:T(8,128)S(1)}, f32[128,1280]{1,0:T(8,128)}, u32[]{:S(2)}) copy-start(f32[128,1280]{1,0:T(8,128)} %copy-done.1) | copy-start | bytes 1966084
Sparse Core Ops, SparseCore 0:
  39.8 72.9 all-gather.3
where the time goes:
time: 238 us; the launch traced here: 237 us
  waiting for transfers between devices  102 us (43%)
  Pallas kernels  41.6 us (17%)
  between operations  24.2 us (10%)
  local copies, waits for them, and re-layouts  22.7 us (10%)
  other arithmetic  18.8 us (8%)
  matrix products  16.5 us (7%)
  starting transfers between devices  11.5 us (5%)
    all_gather x1, waiting for transfers between devices, body(): gathered = lax.all_gather(kv_ext, 'seq', axis=0, tiled=False)  69.2 us
    pallas_call x1, Pallas kernels, flash_attend(): pl.pallas_call(functools.partial(attend_kernel, factor=factor, half=half)...  41.6 us
    ppermute x6, waiting for transfers between devices, gather_rows(): parts.append(lax.ppermute(part, axis, pairs))  18 us
    ppermute x6, waiting for transfers between devices, scatter_sum(): total = total + lax.ppermute(send, axis, pairs).astype(jnp.float32)  14.9 us
    scatter x2, local copies, waits for them, and re-layouts, gather_rows(): jnp.zeros_like(stacked).at[order].set(stacked).reshape(-1, *part.shape[1:])  6.87 us
    dot_general x1, matrix products, body(): jnp.einsum('td,dkf->tkf', mid_rows, up_proj, preferred_element_type=jnp.f...  6.72 us
    ppermute x6, starting transfers between devices, scatter_sum(): total = total + lax.ppermute(send, axis, pairs).astype(jnp.float32)  6.07 us
    ppermute x6, starting transfers between devices, gather_rows(): parts.append(lax.ppermute(part, axis, pairs))  5.36 us
  transfers between devices with their start and end apart: 13, of which 10 were waited for; matrix products, arithmetic and copies ran while one was open for 6% of the time, Pallas kernels for 0%

commit v1 on v0

--- a/solution.py
+++ b/solution.py
@@ -22,13 +22,14 @@
 def gather_rows(part, axis):
     count = lax.axis_size(axis)
     index = lax.axis_index(axis)
-    parts = [part]
+    rows = part.shape[0]
+    out = jnp.zeros((count * rows, *part.shape[1:]), part.dtype)
+    out = lax.dynamic_update_slice_in_dim(out, part, index * rows, 0)
     for shift in range(1, count):
         pairs = [(j, (j + shift) % count) for j in range(count)]
-        parts.append(lax.ppermute(part, axis, pairs))
-    stacked = jnp.stack(parts)
-    order = (index - jnp.arange(count)) % count
-    return jnp.zeros_like(stacked).at[order].set(stacked).reshape(-1, *part.shape[1:])
+        came = lax.ppermute(part, axis, pairs)
+        out = lax.dynamic_update_slice_in_dim(out, came, ((index - shift) % count) * rows, 0)
+    return out
 
 
 def scatter_sum(whole, axis):
@@ -57,10 +58,11 @@
     tiles = rows // Q_TILE
     first = bounds_ref[2 * tiles]
     key_lane = lax.broadcasted_iota(jnp.int32, (K_TILE, lanes), 1)
+    held = {}
     for head in range(heads):
         scale = scale_ref[head]
         for tile in range(tiles):
-            q_raw = proj_ref[tile * Q_TILE : (tile + 1) * Q_TILE, head * 2 * lanes : head * 2 * lanes + lanes]
+            q_raw = proj_ref[tile * Q_TILE : (tile + 1) * Q_TILE, head * lanes : (head + 1) * lanes]
             q_tile = (
                 q_raw * lax.rsqrt(jnp.sum(q_raw * q_raw, axis=1, keepdims=True) + EPSILON) * scale
             ).astype(jnp.bfloat16)
@@ -102,9 +104,20 @@
             top, total, acc = lax.fori_loop(
                 bounds_ref[tile], bounds_ref[tiles + tile] + 1, step, start
             )
-            out_ref[tile * Q_TILE : (tile + 1) * Q_TILE, head * lanes : (head + 1) * lanes] = (
-                acc / total
-            ).astype(out_ref.dtype)
+            result = acc / total
+            pair = head // 2
+            rows_at = slice(tile * Q_TILE, (tile + 1) * Q_TILE)
+            if head % 2 == 0:
+                held[tile] = pltpu.roll(result, half, 1)
+                if head == heads - 1:
+                    out_ref[rows_at, pair * lanes : (pair + 1) * lanes] = held[tile].astype(
+                        out_ref.dtype
+                    )
+            else:
+                joined = jnp.where(
+                    lax.broadcasted_iota(jnp.int32, (Q_TILE, lanes), 1) < half, held[tile], result
+                )
+                out_ref[rows_at, pair * lanes : (pair + 1) * lanes] = joined.astype(out_ref.dtype)
 
 
 def flash_attend(bounds, proj, gathered, scale_pad, query_segs, key_segs, factor, half):
@@ -114,7 +127,7 @@
     vmem = pl.BlockSpec(memory_space=pltpu.VMEM)
     return pl.pallas_call(
         functools.partial(attend_kernel, factor=factor, half=half),
-        out_shape=jax.ShapeDtypeStruct((rows, heads * lanes), jnp.bfloat16),
+        out_shape=jax.ShapeDtypeStruct((rows, -(-heads // 2) * lanes), jnp.bfloat16),
         in_specs=[pl.BlockSpec(memory_space=pltpu.SMEM)] + [vmem] * 5,
         out_specs=vmem,
         cost_estimate=pl.CostEstimate(
@@ -148,18 +161,27 @@
     state_own = unit_rows(hidden.astype(jnp.float32)).astype(jnp.bfloat16)
     gathered_state = gather_rows(state_own, "tensor")
     lanes = 2 * head_dim
-    weight_pad = jnp.concatenate(
-        [
-            in_proj[:, :, :head_dim],
-            jnp.zeros((model_width, heads_dev, head_dim), in_proj.dtype),
-            in_proj[:, :, head_dim:],
-        ],
-        axis=2,
-    ).reshape(model_width, heads_dev * 2 * lanes)
-    projected = jnp.dot(gathered_state, weight_pad, preferred_element_type=jnp.float32)
+    projected = jnp.dot(
+        gathered_state,
+        in_proj.reshape(model_width, heads_dev * 3 * head_dim),
+        preferred_element_type=jnp.float32,
+    )
+    width = 3 * head_dim
+    query_pad = jnp.concatenate(
+        sum(
+            [
+                [
+                    projected[:, h * width : h * width + head_dim],
+                    jnp.zeros((local_tokens, head_dim), jnp.float32),
+                ]
+                for h in range(heads_dev)
+            ],
+            [],
+        ),
+        axis=1,
+    )
     key_value = jnp.concatenate(
-        [projected[:, (2 * h + 1) * lanes : (2 * h + 2) * lanes] for h in range(heads_dev)],
-        axis=1,
+        [projected[:, h * width + head_dim : (h + 1) * width] for h in range(heads_dev)], axis=1
     ).astype(jnp.bfloat16)
     first_token = seq_index * local_tokens
     seg_rows = -(-local_tokens // channels)
@@ -186,7 +208,7 @@
     bounds = jnp.concatenate([block_lo, block_hi, first_token[None]]).astype(jnp.int32)
     heads_pad = flash_attend(
         bounds,
-        projected,
+        query_pad,
         gathered,
         scale_pad,
         segment_ids.reshape(local_tokens, 1),
@@ -194,9 +216,7 @@
         math.sqrt(head_dim),
         head_dim,
     )
-    out_pad = jnp.pad(
-        out_proj.reshape(heads_dev, head_dim, model_width), ((0, 0), (head_dim, 0), (0, 0))
-    ).reshape(heads_dev * lanes, model_width)
+    heads_flat = heads_pad[:, : heads_dev * head_dim]
     slots_dev = page_slot.shape[0] // seq_count
     my_slots = seq_index * slots_dev + jnp.arange(slots_dev, dtype=jnp.int32)
     page_ids = jnp.arange(page_slot.shape[0], dtype=jnp.int32)
@@ -213,9 +233,9 @@
             for j in range(slots_dev)
         ]
     )
-    chosen = heads_pad
+    chosen = heads_flat
     attn_own = scatter_sum(
-        jnp.dot(chosen, out_pad, preferred_element_type=jnp.float32).astype(jnp.bfloat16),
+        jnp.dot(chosen, out_proj, preferred_element_type=jnp.float32).astype(jnp.bfloat16),
         "tensor",
     )
     state_f = state_own.astype(jnp.float32)

time: 238 us -> 234 us (0.983)
  other arithmetic: 18.8 us -> 13 us
  Pallas kernels: 41.6 us -> 46.2 us
  waiting for transfers between devices: 102 us -> 105 us
    scatter x2 -> x0, local copies, waits for them, and re-layouts: 6.87 us -> none  [gather_rows(): jnp.zeros_like(stacked).at[order].set(stacked).reshape(-1, *part.shape[1:])]
    dynamic_update_slice x0 -> x6, local copies, waits for them, and re-layouts: none -> 5.25 us  [gather_rows(): lax.dynamic_update_slice_in_dim(out, came, (index - shift) % count * rows...]
    pallas_call x1, Pallas kernels: 41.6 us -> 46.2 us  [flash_attend(): pl.pallas_call(functools.partial(attend_kernel, factor=factor, half=half)...]
    ppermute x6, waiting for transfers between devices: 18 us -> 22.3 us  [gather_rows(): came = lax.ppermute(part, axis, pairs)]
    another operation x4 -> x0, other arithmetic: 3.9 us -> none  [gather_rows(): stacked = jnp.stack(parts)]
    concatenate x1 -> x0, other arithmetic: 3.54 us -> none  [body(): jnp.concatenate([in_proj[:, :, :head_dim], jnp.zeros((model_width, heads_...]
    reduce_sum x5, other arithmetic: 4.98 us -> 7.59 us  [unit_rows(): jnp.sum(matrix * matrix, axis=-1, keepdims=True) + EPSILON]
  transfers between devices with their start and end apart: 13 -> 13, of which waited for: 10 -> 11; matrix products, arithmetic and copies ran while one was open for 6% -> 5% of each run, Pallas kernels for 0% -> 0%
where the time goes in v1:
time: 234 us; the launch traced here: 235 us
  waiting for transfers between devices  105 us (45%)
  Pallas kernels  46.2 us (20%)
  between operations  24.5 us (10%)
  local copies, waits for them, and re-layouts  20.5 us (9%)
  matrix products  14.2 us (6%)
  other arithmetic  13 us (6%)
  starting transfers between devices  11.6 us (5%)
    all_gather x1, waiting for transfers between devices, body(): gathered = lax.all_gather(kv_ext, 'seq', axis=0, tiled=False)  67.9 us
    pallas_call x1, Pallas kernels, flash_attend(): pl.pallas_call(functools.partial(attend_kernel, factor=factor, half=half)...  46.2 us
    ppermute x6, waiting for transfers between devices, gather_rows(): came = lax.ppermute(part, axis, pairs)  22.3 us
    ppermute x6, waiting for transfers between devices, scatter_sum(): total = total + lax.ppermute(send, axis, pairs).astype(jnp.float32)  15.2 us
    reduce_sum x5, other arithmetic, unit_rows(): jnp.sum(matrix * matrix, axis=-1, keepdims=True) + EPSILON  7.59 us
    dot_general x1, matrix products, body(): jnp.einsum('td,dkf->tkf', mid_rows, up_proj, preferred_element_type=jnp.f...  6.36 us
    ppermute x6, starting transfers between devices, scatter_sum(): total = total + lax.ppermute(send, axis, pairs).astype(jnp.float32)  5.99 us
    ppermute x6, starting transfers between devices, gather_rows(): came = lax.ppermute(part, axis, pairs)  5.6 us
  transfers between devices with their start and end apart: 13, of which 11 were waited for; matrix products, arithmetic and copies ran while one was open for 5% of the time, Pallas kernels for 0%

profile of v1, /device:TPU:26, one launch (start us, length us, event | category | flops | bytes accessed | tf_op | source)
XLA Modules:
  0.0 235.5 jit_solution(5053686865575211692)
XLA Ops:
  7.2 0.0 copy-start
  7.2 0.0 all-gather.4.cloned.1.call-start
  7.2 1.3 fusion.9
  8.5 1.2 broadcast.77.clone
  9.7 0.9 constant_dynamic-update-slice_fusion.7
  10.6 1.6 collective-permute-start.1
  12.2 1.4 collective-permute-start.2
  13.7 0.0 copy-start.11
  13.7 6.7 %collective-permute-done = bf16[128,1280]{1,0:T(8,128)(2,1)} collective-permute-done((bf16[128,1280]{1,0:T(8,128)(2,1)}, bf16[128,1280]{1,0:T(8,128)(2,1)}, u32[]{:S(2)}, u32[]{:S(2)}) %collective-permute-start) | collective-permute-done | bytes 327712 | tf_op jit(solution)/shard_map/ppermute | solution.py:30
  20.4 1.7 constant_dynamic-update-slice_fusion.6
  22.1 1.7 constant_dynamic-update-slice_fusion.5
  23.9 3.2 %collective-permute-done.2 = bf16[128,1280]{1,0:T(8,128)(2,1)} collective-permute-done((bf16[128,1280]{1,0:T(8,128)(2,1)}, bf16[128,1280]{1,0:T(8,128)(2,1)}, u32[]{:S(2)}, u32[]{:S(2)}) %collective-permute-start.2) | collective-permute-done | bytes 327712 | tf_op jit(solution)/shard_map/ppermute | solution.py:30
  27.0 1.7 constant_dynamic-update-slice_fusion.4
  28.8 3.7 %fusion.24 = (bf16[512,768]{1,0:T(8,128)(2,1)S(1)}, f32[512,768]{1,0:T(8,128)}) fusion(bf16[512,1280]{1,0:T(8,128)(2,1)} %constant_dynamic-update-slice_fusion.4, bf16[1280,768]{0,1:T(8,128)(2,1)S(1)} %bitcast.77), kind=kOutput, calls=%fused_computation.79 | convolution fusion | flops 1007026176 | bytes 5636096 | tf_op jit(solution)/shard_map/dot_general | solution.py:164
  32.5 0.1 fusion.22
  32.6 0.9 maximum_bitcast_fusion
  33.5 0.0 all-gather.4.cloned.1.call-update
  33.6 0.8 copy.20.qseg_ref
  34.4 0.6 pad.4
  35.0 0.1 slice_reduce_fusion.4
  35.1 2.3 fusion.21
  37.5 2.4 %concatenate.16.proj_ref = f32[512,512]{1,0:T(8,128)} concatenate(f32[512,64]{1,0:T(8,128)} %get-tuple-element.23, f32[512,64]{1,0:T(8,128)S(1)} %broadcast.81, f32[512,64]{1,0:T(8,128)} %get-tuple-element.22, f32[512,64]{1,0:T(8,128)S(1)} %broadcast.81, f32[512,64]{1,0:T(8,128)} %get-tuple-element.21, f32[512,64]{1,0:T(8,128)S(1)} %broadcast.81, f32[512,64]{1,0:T(8,128)} %get-tuple-element.20, ...), dimensions={1} | concatenate | bytes 2097152 | tf_op jit(solution)/shard_map/concatenate | solution.py:170
  39.8 67.9 %all-gather.4.cloned.1.call-done.kv_ref = bf16[8,513,512]{2,1,0:T(8,128)(2,1)} async-done(((bf16[1,513,512]{2,1,0:T(8,128)(2,1)}), bf16[8,513,512]{2,1,0:T(8,128)(2,1)}) %all-gather.4.cloned.1.call-update) | async-done | bytes 4202512 | tf_op jit(solution)/shard_map/all_gather | solution.py:192
  107.8 0.9 fusion.20
  108.6 0.6 convert.17.kseg_ref
  109.3 0.2 convert_reduce_fusion
  109.5 0.2 fusion.16
  109.6 0.6 pad_add_fusion.bounds_ref
  110.2 46.2 %shard_map.113 = bf16[512,256]{1,0:T(8,128)(2,1)} custom-call(s32[5]{0:T(128)} %pad_add_fusion.bounds_ref, f32[512,512]{1,0:T(8,128)} %concatenate.16.proj_ref, bf16[8,513,512]{2,1,0:T(8,128)(2,1)} %all-gather.4.cloned.1.call-done.kv_ref, f32[4,1,128]{2,1,0:T(1,128)} %bitcast.76, s32[512,1]{1,0:T(8,128)} %copy.20.qseg_ref, s32[1,4096]{1,0:T(1,128)} %convert.17.kseg_ref), custom_call_target="tpu_custom_call" | custom-call | flops 4294967296 | bytes 4194304 | tf_op jit(solution)/shard_map/pallas_call | solution.py:128
  156.4 1.7 convolution_convert_fusion.1
  158.1 1.0 copy-done.1
  159.2 1.0 dynamic-slice_bitcast_fusion.5
  160.2 1.5 collective-permute-start.4
  161.6 1.4 collective-permute-start.5
  163.1 6.8 %collective-permute-done.3 = bf16[128,1280]{1,0:T(8,128)(2,1)} collective-permute-done((bf16[128,1280]{1,0:T(8,128)(2,1)}, bf16[128,1280]{1,0:T(8,128)(2,1)}, u32[]{:S(2)}, u32[]{:S(2)}) %collective-permute-start.3) | collective-permute-done | bytes 327712 | tf_op jit(solution)/shard_map/ppermute | solution.py:43
  169.9 1.1 collective-permute-done.4
  171.0 5.4 %collective-permute-done.5 = bf16[128,1280]{1,0:T(8,128)(2,1)} collective-permute-done((bf16[128,1280]{1,0:T(8,128)(2,1)}, bf16[128,1280]{1,0:T(8,128)(2,1)}, u32[]{:S(2)}, u32[]{:S(2)}) %collective-permute-start.5) | collective-permute-done | bytes 327712 | tf_op jit(solution)/shard_map/ppermute | solution.py:43
  176.5 1.5 multiply_reduce_fusion.3
  178.0 1.8 multiply_reduce_fusion.2
  179.8 0.0 copy-start.9
  179.8 0.1 broadcast.77
  179.9 0.1 constant_dynamic-update-slice_fusion.3
  180.1 0.6 copy-done.2
  180.7 0.9 collective-permute-start.6
  181.5 0.2 select_reduce_fusion
  181.7 1.5 collective-permute-start.7
  183.3 0.2 collective-permute-start.8
  183.5 5.8 %collective-permute-done.6 = bf16[128,1280]{1,0:T(8,128)(2,1)S(1)} collective-permute-done((bf16[128,1280]{1,0:T(8,128)(2,1)S(1)}, bf16[128,1280]{1,0:T(8,128)(2,1)S(1)}, u32[]{:S(2)}, u32[]{:S(2)}) %collective-permute-start.6) | collective-permute-done | bytes 327712 | tf_op jit(solution)/shard_map/ppermute | solution.py:30
  189.3 3.1 %collective-permute-done.7 = bf16[128,1280]{1,0:T(8,128)(2,1)S(1)} collective-permute-done((bf16[128,1280]{1,0:T(8,128)(2,1)S(1)}, bf16[128,1280]{1,0:T(8,128)(2,1)S(1)}, u32[]{:S(2)}, u32[]{:S(2)}) %collective-permute-start.7) | collective-permute-done | bytes 327712 | tf_op jit(solution)/shard_map/ppermute | solution.py:30
  192.5 3.5 %collective-permute-done.8 = bf16[128,1280]{1,0:T(8,128)(2,1)S(1)} collective-permute-done((bf16[128,1280]{1,0:T(8,128)(2,1)S(1)}, bf16[128,1280]{1,0:T(8,128)(2,1)S(1)}, u32[]{:S(2)}, u32[]{:S(2)}) %collective-permute-start.8) | collective-permute-done | bytes 327712 | tf_op jit(solution)/shard_map/ppermute | solution.py:30
  196.0 6.4 %fusion = f32[512,2,1280]{2,0,1:T(8,128)S(1)} fusion(bf16[1280,2,1280]{2,1,0:T(2,128)(2,1)} %param.15, bf16[512,1280]{1,0:T(8,128)(2,1)S(1)} %constant_dynamic-update-slice_fusion), kind=kOutput, calls=%fused_computation | convolution fusion | flops 3355443200 | bytes 13107200 | tf_op jit(solution)/shard_map/td,dkf->tkf/dot_general | solution.py:244
  202.4 2.4 %convolution_convert_fusion = bf16[512,1280]{1,0:T(8,128)(2,1)S(1)} fusion(bf16[1280,1280]{1,0:T(8,128)(2,1)S(1)} %copy-done, f32[512,2,1280]{2,0,1:T(8,128)S(1)} %fusion, f32[1280]{0:T(1024)S(1)} %get-tuple-element.5, f32[1280]{0:T(1024)S(1)} %get-tuple-element.4), kind=kOutput, calls=%fused_computation.2 | convolution fusion | flops 1684275200 | bytes 9840640 | tf_op jit(solution)/shard_map/dot_general | solution.py:250
  204.8 1.0 copy-done.4
  205.9 0.9 dynamic-slice_bitcast_fusion.2
  206.8 1.5 collective-permute-start.10
  208.3 1.6 collective-permute-start.11
  209.9 0.7 fusion.23
  220.7 1.4 constant_dynamic-slice_fusion.3
  222.1 0.9 pad_maximum_fusion
  223.0 0.6 collective-permute-done.11
  223.6 1.2 collective-permute-done.9
  224.8 1.4 multiply_reduce_fusion.1
  226.2 1.6 multiply_reduce_fusion
  227.8 0.9 multiply_convert_fusion
  (42 shorter events, 0.3 us)
Async XLA Ops:
  7.2 195.2 %copy-start = (bf16[1280,1280]{1,0:T(8,128)(2,1)S(1)}, bf16[1280,1280]{1,0:T(8,128)(2,1)}, u32[]{:S(2)}) copy-start(bf16[1280,1280]{1,0:T(8,128)(2,1)} %param.16) | copy-start | bytes 9830404
  7.2 100.6 %all-gather.4.cloned.1.call-start = ((), (), s32[]{:S(2)}) async-start(), calls=%async_computation | async-start | bytes 4792320 | tf_op jit(solution)/shard_map/all_gather | solution.py:192
  7.2 6.4 %copy-start.7 = (s32[512]{0:T(512)S(1)}, s32[512]{0:T(512)}, u32[]{:S(2)}) copy-start(s32[512]{0:T(512)} %param.11) | copy-start | bytes 6148
  8.5 1.2 copy-start.6
  10.6 9.8 %collective-permute-start = (bf16[128,1280]{1,0:T(8,128)(2,1)}, bf16[128,1280]{1,0:T(8,128)(2,1)}, u32[]{:S(2)}, u32[]{:S(2)}) collective-permute-start(bf16[128,1280]{1,0:T(8,128)(2,1)} %get-tuple-element.13), channel_id=1, source_target_pairs={{0,1},{1,2},{2,3},{3,0},{4,5},{5,6},{6,7},{7,4},{8,9},{9,10},{10,1... | collective-permute-start | bytes 983048 | tf_op jit(solution)/shard_map/ppermute | solution.py:30
  10.6 11.5 %collective-permute-start.1 = (bf16[128,1280]{1,0:T(8,128)(2,1)}, bf16[128,1280]{1,0:T(8,128)(2,1)}, u32[]{:S(2)}, u32[]{:S(2)}) collective-permute-start(bf16[128,1280]{1,0:T(8,128)(2,1)} %get-tuple-element.13), channel_id=1, source_target_pairs={{0,2},{1,3},{2,0},{3,1},{4,6},{5,7},{6,4},{7,5},{8,10},{9,11},{10,... | collective-permute-start | bytes 983048 | tf_op jit(solution)/shard_map/ppermute | solution.py:30
  12.2 14.8 %collective-permute-start.2 = (bf16[128,1280]{1,0:T(8,128)(2,1)}, bf16[128,1280]{1,0:T(8,128)(2,1)}, u32[]{:S(2)}, u32[]{:S(2)}) collective-permute-start(bf16[128,1280]{1,0:T(8,128)(2,1)} %get-tuple-element.13), channel_id=1, source_target_pairs={{0,3},{1,0},{2,1},{3,2},{4,7},{5,4},{6,5},{7,6},{8,11},{9,8},{10,9... | collective-permute-start | bytes 983048 | tf_op jit(solution)/shard_map/ppermute | solution.py:30
  13.7 15.1 %copy-start.11 = (bf16[1280,4,192]{0,2,1:T(8,128)(2,1)S(1)}, bf16[1280,4,192]{0,2,1:T(8,128)(2,1)}, u32[]{:S(2)}) copy-start(bf16[1280,4,192]{0,2,1:T(8,128)(2,1)} %param.13) | copy-start | bytes 5898244
  32.5 1.9 copy-start.10
  158.1 1.1 copy-start.1
  158.1 4.9 %copy-start.8 = (f32[2,1280]{1,0:T(2,128)S(1)}, f32[2,1280]{1,0:T(2,128)}, u32[]{:S(2)}) copy-start(f32[2,1280]{1,0:T(2,128)} %param.19) | copy-start | bytes 30724
  160.2 9.8 %collective-permute-start.3 = (bf16[128,1280]{1,0:T(8,128)(2,1)}, bf16[128,1280]{1,0:T(8,128)(2,1)}, u32[]{:S(2)}, u32[]{:S(2)}) collective-permute-start(bf16[128,1280]{1,0:T(8,128)(2,1)} %get-tuple-element.27), channel_id=1, source_target_pairs={{0,1},{1,2},{2,3},{3,0},{4,5},{5,6},{6,7},{7,4},{8,9},{9,10},{10,1... | collective-permute-start | bytes 983048 | tf_op jit(solution)/shard_map/ppermute | solution.py:43
  160.2 10.9 %collective-permute-start.4 = (bf16[128,1280]{1,0:T(8,128)(2,1)}, bf16[128,1280]{1,0:T(8,128)(2,1)}, u32[]{:S(2)}, u32[]{:S(2)}) collective-permute-start(bf16[128,1280]{1,0:T(8,128)(2,1)} %get-tuple-element.29), channel_id=1, source_target_pairs={{0,2},{1,3},{2,0},{3,1},{4,6},{5,7},{6,4},{7,5},{8,10},{9,11},{10,... | collective-permute-start | bytes 983048 | tf_op jit(solution)/shard_map/ppermute | solution.py:43
  161.6 14.8 %collective-permute-start.5 = (bf16[128,1280]{1,0:T(8,128)(2,1)}, bf16[128,1280]{1,0:T(8,128)(2,1)}, u32[]{:S(2)}, u32[]{:S(2)}) collective-permute-start(bf16[128,1280]{1,0:T(8,128)(2,1)} %get-tuple-element.28), channel_id=1, source_target_pairs={{0,3},{1,0},{2,1},{3,2},{4,7},{5,4},{6,5},{7,6},{8,11},{9,8},{10,9... | collective-permute-start | bytes 983048 | tf_op jit(solution)/shard_map/ppermute | solution.py:43
  179.8 0.9 copy-start.2
  179.8 1.7 copy-start.12
  179.8 3.4 %copy-start.9 = (f32[2,1280]{1,0:T(2,128)S(1)}, f32[2,1280]{1,0:T(2,128)}, u32[]{:S(2)}) copy-start(f32[2,1280]{1,0:T(2,128)} %param.18) | copy-start | bytes 30724
  180.7 8.6 %collective-permute-start.6 = (bf16[128,1280]{1,0:T(8,128)(2,1)S(1)}, bf16[128,1280]{1,0:T(8,128)(2,1)S(1)}, u32[]{:S(2)}, u32[]{:S(2)}) collective-permute-start(bf16[128,1280]{1,0:T(8,128)(2,1)S(1)} %get-tuple-element.9), channel_id=1, source_target_pairs={{0,1},{1,2},{2,3},{3,0},{4,5},{5,6},{6,7},{7,4},{8,9},{9,10},{10,1... | collective-permute-start | bytes 983048 | tf_op jit(solution)/shard_map/ppermute | solution.py:30
  181.7 10.7 %collective-permute-start.7 = (bf16[128,1280]{1,0:T(8,128)(2,1)S(1)}, bf16[128,1280]{1,0:T(8,128)(2,1)S(1)}, u32[]{:S(2)}, u32[]{:S(2)}) collective-permute-start(bf16[128,1280]{1,0:T(8,128)(2,1)S(1)} %get-tuple-element.9), channel_id=1, source_target_pairs={{0,2},{1,3},{2,0},{3,1},{4,6},{5,7},{6,4},{7,5},{8,10},{9,11},{10,... | collective-permute-start | bytes 983048 | tf_op jit(solution)/shard_map/ppermute | solution.py:30
  183.3 12.7 %collective-permute-start.8 = (bf16[128,1280]{1,0:T(8,128)(2,1)S(1)}, bf16[128,1280]{1,0:T(8,128)(2,1)S(1)}, u32[]{:S(2)}, u32[]{:S(2)}) collective-permute-start(bf16[128,1280]{1,0:T(8,128)(2,1)S(1)} %get-tuple-element.9), channel_id=1, source_target_pairs={{0,3},{1,0},{2,1},{3,2},{4,7},{5,4},{6,5},{7,6},{8,11},{9,8},{10,9... | collective-permute-start | bytes 983048 | tf_op jit(solution)/shard_map/ppermute | solution.py:30
  204.8 1.1 copy-start.4
  206.8 16.1 %collective-permute-start.10 = (bf16[128,1280]{1,0:T(8,128)(2,1)}, bf16[128,1280]{1,0:T(8,128)(2,1)}, u32[]{:S(2)}, u32[]{:S(2)}) collective-permute-start(bf16[128,1280]{1,0:T(8,128)(2,1)} %get-tuple-element.26), channel_id=1, source_target_pairs={{0,2},{1,3},{2,0},{3,1},{4,6},{5,7},{6,4},{7,5},{8,10},{9,11},{10,... | collective-permute-start | bytes 983048 | tf_op jit(solution)/shard_map/ppermute | solution.py:43
  208.3 15.3 %collective-permute-start.11 = (bf16[128,1280]{1,0:T(8,128)(2,1)}, bf16[128,1280]{1,0:T(8,128)(2,1)}, u32[]{:S(2)}, u32[]{:S(2)}) collective-permute-start(bf16[128,1280]{1,0:T(8,128)(2,1)} %get-tuple-element.25), channel_id=1, source_target_pairs={{0,3},{1,0},{2,1},{3,2},{4,7},{5,4},{6,5},{7,6},{8,11},{9,8},{10,9... | collective-permute-start | bytes 983048 | tf_op jit(solution)/shard_map/ppermute | solution.py:43
  209.9 14.8 %collective-permute-start.9 = (bf16[128,1280]{1,0:T(8,128)(2,1)}, bf16[128,1280]{1,0:T(8,128)(2,1)}, u32[]{:S(2)}, u32[]{:S(2)}) collective-permute-start(bf16[128,1280]{1,0:T(8,128)(2,1)} %get-tuple-element.24), channel_id=1, source_target_pairs={{0,1},{1,2},{2,3},{3,0},{4,5},{5,6},{6,7},{7,4},{8,9},{9,10},{10,1... | collective-permute-start | bytes 983048 | tf_op jit(solution)/shard_map/ppermute | solution.py:43
  220.7 4.0 %copy-start.5 = (bf16[512,1280]{1,0:T(8,128)(2,1)S(1)}, bf16[512,1280]{1,0:T(8,128)(2,1)}, u32[]{:S(2)}) copy-start(bf16[512,1280]{1,0:T(8,128)(2,1)} %copy-done.4) | copy-start | bytes 3932164
  222.1 4.1 %copy-start.3 = (f32[128,1280]{1,0:T(8,128)S(1)}, f32[128,1280]{1,0:T(8,128)}, u32[]{:S(2)}) copy-start(f32[128,1280]{1,0:T(8,128)} %copy-done.2) | copy-start | bytes 1966084
Sparse Core Ops, SparseCore 0:
  33.7 74.0 all-gather.3

commit v2 on v1

--- a/solution.py
+++ b/solution.py
@@ -20,6 +20,24 @@
 
 
 def gather_rows(part, axis):
+    count = lax.axis_size(axis)
+    index = lax.axis_index(axis)
+    if count & (count - 1):
+        return gather_rows_ring(part, axis)
+    held = part
+    bit = 1
+    while bit < count:
+        pairs = [(j, j ^ bit) for j in range(count)]
+        came = lax.ppermute(held, axis, pairs)
+        low = (index & bit) == 0
+        held = jnp.concatenate(
+            [jnp.where(low, held, came), jnp.where(low, came, held)], axis=0
+        )
+        bit *= 2
+    return held
+
+
+def gather_rows_ring(part, axis):
     count = lax.axis_size(axis)
     index = lax.axis_index(axis)
     rows = part.shape[0]
@@ -33,6 +51,24 @@
 
 
 def scatter_sum(whole, axis):
+    count = lax.axis_size(axis)
+    index = lax.axis_index(axis)
+    if count & (count - 1):
+        return scatter_sum_ring(whole, axis)
+    held = whole.reshape(count, whole.shape[0] // count, *whole.shape[1:])
+    bit = 1
+    while bit < count:
+        pairs = [(j, j ^ bit) for j in range(count)]
+        halves = held.reshape(held.shape[0] // 2, 2, *held.shape[1:])
+        low = (index & bit) == 0
+        keep = jnp.where(low, halves[:, 0], halves[:, 1])
+        send = jnp.where(low, halves[:, 1], halves[:, 0])
+        held = keep.astype(jnp.float32) + lax.ppermute(send, axis, pairs).astype(jnp.float32)
+        bit *= 2
+    return held[0]
+
+
+def scatter_sum_ring(whole, axis):
     count = lax.axis_size(axis)
     index = lax.axis_index(axis)
     blocks = whole.reshape(count, whole.shape[0] // count, *whole.shape[1:])

time: 234 us -> 236 us (level)
  the two profiles are of different devices: /device:TPU:26 before, /device:TPU:18 now
where the time goes in v2:
time: 236 us
  waiting for transfers between devices  124 us (53%)
  Pallas kernels  41.5 us (18%)
  between operations  24.5 us (10%)
  other arithmetic  15.8 us (7%)
  matrix products  12.9 us (5%)
  local copies, waits for them, and re-layouts  11.2 us (5%)
  starting transfers between devices  6.31 us (3%)
    all_gather x1, waiting for transfers between devices, body(): gathered = lax.all_gather(kv_ext, 'seq', axis=0, tiled=False)  67.3 us
    pallas_call x1, Pallas kernels, flash_attend(): pl.pallas_call(functools.partial(attend_kernel, factor=factor, half=half)...  41.5 us
    ppermute x4, waiting for transfers between devices, gather_rows(): came = lax.ppermute(held, axis, pairs)  34.4 us
    ppermute x4, waiting for transfers between devices, scatter_sum(): lax.ppermute(send, axis, pairs).astype(jnp.float32)  21.8 us
    dot_general x1, matrix products, body(): jnp.einsum('td,dkf->tkf', mid_rows, up_proj, preferred_element_type=jnp.f...  6.36 us
  transfers between devices with their start and end apart: 9, of which 9 were waited for; matrix products, arithmetic and copies ran while one was open for 4% of the time, Pallas kernels for 0%

profile of v2, /device:TPU:18, one launch (start us, length us, event | category | flops | bytes accessed | tf_op | source)
XLA Modules:
  0.0 235.8 jit_solution(420044830133909232)
XLA Ops:
  7.2 0.0 copy-start
  7.2 0.0 all-gather.4.cloned.1.call-start
  7.2 1.3 fusion.16
  8.5 1.8 fusion.17
  10.3 2.0 collective-permute-done
  12.3 1.3 broadcast_select_fusion.7
  13.6 0.0 copy-start.7
  13.6 0.0 copy-start.8
  13.6 0.7 copy-done.7
  14.3 0.9 pad_maximum_fusion
  15.2 1.5 collective-permute-start.1
  16.7 15.5 %collective-permute-done.1 = bf16[256,1280]{1,0:T(8,128)(2,1)} collective-permute-done((bf16[256,1280]{1,0:T(8,128)(2,1)}, bf16[256,1280]{1,0:T(8,128)(2,1)}, u32[]{:S(2)}, u32[]{:S(2)}) %collective-permute-start.1) | collective-permute-done | bytes 655392 | tf_op jit(solution)/shard_map/ppermute | solution.py:31
  32.3 1.5 broadcast_select_fusion.3
  33.8 2.4 %fusion.33 = (bf16[512,768]{1,0:T(8,128)(2,1)S(1)}, f32[512,768]{1,0:T(8,128)}) fusion(bf16[1280,768]{0,1:T(8,128)(2,1)S(1)} %bitcast.124, bf16[256,1280]{1,0:T(8,128)(2,1)S(1)} %get-tuple-element.23, bf16[256,1280]{1,0:T(8,128)(2,1)S(1)} %get-tuple-element.22), kind=kOutput, calls=%fused_computation.97 | convolution fusion | flops 1009647616 | bytes 5636096 | tf_op jit(solution)/shard_map/dot_general | solution.py:200
  36.2 0.1 fusion.31
  36.4 0.9 maximum_bitcast_fusion.2
  37.2 0.0 all-gather.4.cloned.1.call-update
  37.3 0.9 copy.34.qseg_ref
  38.1 0.6 pad.4
  38.7 0.1 slice_reduce_fusion.4
  38.8 2.3 fusion.30
  41.2 2.4 %concatenate.30.proj_ref = f32[512,512]{1,0:T(8,128)} concatenate(f32[512,64]{1,0:T(8,128)} %get-tuple-element.19, f32[512,64]{1,0:T(8,128)S(1)} %broadcast.113, f32[512,64]{1,0:T(8,128)} %get-tuple-element.18, f32[512,64]{1,0:T(8,128)S(1)} %broadcast.113, f32[512,64]{1,0:T(8,128)} %get-tuple-element.17, f32[512,64]{1,0:T(8,128)S(1)} %broadcast.113, ...), dimensions={1} | concatenate | bytes 2097152 | tf_op jit(solution)/shard_map/concatenate | solution.py:206
  43.6 67.3 %all-gather.4.cloned.1.call-done.kv_ref = bf16[8,513,512]{2,1,0:T(8,128)(2,1)} async-done(((bf16[1,513,512]{2,1,0:T(8,128)(2,1)}), bf16[8,513,512]{2,1,0:T(8,128)(2,1)}) %all-gather.4.cloned.1.call-update) | async-done | bytes 4202512 | tf_op jit(solution)/shard_map/all_gather | solution.py:228
  110.9 0.9 fusion.29
  111.8 0.6 convert.17.kseg_ref
  112.4 0.2 convert_reduce_fusion
  112.6 0.2 fusion.24
  112.8 0.6 pad_add_fusion.bounds_ref
  113.4 41.5 %shard_map.113 = bf16[512,256]{1,0:T(8,128)(2,1)} custom-call(s32[5]{0:T(128)} %pad_add_fusion.bounds_ref, f32[512,512]{1,0:T(8,128)} %concatenate.30.proj_ref, bf16[8,513,512]{2,1,0:T(8,128)(2,1)} %all-gather.4.cloned.1.call-done.kv_ref, f32[4,1,128]{2,1,0:T(1,128)} %bitcast.123, s32[512,1]{1,0:T(8,128)} %copy.34.qseg_ref, s32[1,4096]{1,0:T(1,128)} %convert.17.kseg_ref), custom_call_target="tpu_custom_call" | custom-call | flops 4294967296 | bytes 4194304 | tf_op jit(solution)/shard_map/pallas_call | solution.py:164
  154.9 1.7 convolution_convert_fusion.1
  156.6 0.1 select_bitcast_fusion.3
  156.7 0.1 collective-permute-start.2
  156.7 2.1 collective-permute-done.2
  158.8 0.2 fusion.14
  159.0 0.0 copy-start.10
  159.1 0.1 select_bitcast_fusion.2
  159.1 1.5 collective-permute-start.3
  160.7 15.3 %collective-permute-done.3 = f32[1,128,1280]{2,1,0:T(8,128)S(1)} collective-permute-done((f32[1,128,1280]{2,1,0:T(8,128)S(1)}, f32[1,128,1280]{2,1,0:T(8,128)S(1)}, u32[]{:S(2)}, u32[]{:S(2)}) %collective-permute-start.3) | collective-permute-done | bytes 655392 | tf_op jit(solution)/shard_map/ppermute | solution.py:66
  176.0 0.2 fusion.23
  176.2 0.3 multiply_reduce_fusion.1
  176.5 0.3 multiply_convert_fusion.1
  176.8 0.0 copy-start.11
  176.8 0.1 collective-permute-start.4
  176.9 1.6 collective-permute-done.4
  178.6 1.5 collective-permute-start.5
  180.2 15.3 %collective-permute-done.5 = bf16[256,1280]{1,0:T(8,128)(2,1)S(1)} collective-permute-done((bf16[256,1280]{1,0:T(8,128)(2,1)S(1)}, bf16[256,1280]{1,0:T(8,128)(2,1)S(1)}, u32[]{:S(2)}, u32[]{:S(2)}) %collective-permute-start.5) | collective-permute-done | bytes 655392 | tf_op jit(solution)/shard_map/ppermute | solution.py:31
  195.4 0.2 broadcast_select_fusion.1
  195.7 6.4 %fusion = f32[512,2,1280]{2,0,1:T(8,128)S(1)} fusion(bf16[1280,2,1280]{2,1,0:T(2,128)(2,1)} %param.15, bf16[256,1280]{1,0:T(8,128)(2,1)S(1)} %get-tuple-element.21, bf16[256,1280]{1,0:T(8,128)(2,1)S(1)} %get-tuple-element.20), kind=kOutput, calls=%fused_computation | convolution fusion | flops 3358064640 | bytes 13107200 | tf_op jit(solution)/shard_map/td,dkf->tkf/dot_general | solution.py:280
  202.0 2.5 %convolution_convert_fusion = bf16[512,1280]{1,0:T(8,128)(2,1)S(1)} fusion(bf16[1280,1280]{1,0:T(8,128)(2,1)S(1)} %copy-done, f32[512,2,1280]{2,0,1:T(8,128)S(1)} %fusion, f32[1280]{0:T(1024)S(1)} %get-tuple-element.5, f32[1280]{0:T(1024)S(1)} %get-tuple-element.4), kind=kOutput, calls=%fused_computation.2 | convolution fusion | flops 1684275200 | bytes 9840640 | tf_op jit(solution)/shard_map/dot_general | solution.py:286
  204.5 0.1 select_bitcast_fusion.1
  204.6 0.1 collective-permute-start.6
  204.7 2.1 collective-permute-done.6
  206.8 0.2 fusion.13
  207.0 1.0 copy-done.5
  208.1 0.9 select_bitcast_fusion
  209.0 1.5 collective-permute-start.7
  210.5 0.2 select_reduce_fusion
  210.6 0.7 fusion.32
  221.5 1.4 constant_dynamic-slice_fusion.3
  222.8 0.9 pad_maximum_fusion.2
  223.7 2.4 %collective-permute-done.7 = f32[1,128,1280]{2,1,0:T(8,128)} collective-permute-done((f32[1,128,1280]{2,1,0:T(8,128)}, f32[1,128,1280]{2,1,0:T(8,128)}, u32[]{:S(2)}, u32[]{:S(2)}) %collective-permute-start.7) | collective-permute-done | bytes 655392 | tf_op jit(solution)/shard_map/ppermute | solution.py:66
  226.1 1.3 fusion.19
  227.4 0.4 multiply_reduce_fusion
  227.8 1.1 multiply_convert_fusion
  (40 shorter events, 0.3 us)
Async XLA Ops:
  7.2 194.9 %copy-start = (bf16[1280,1280]{1,0:T(8,128)(2,1)S(1)}, bf16[1280,1280]{1,0:T(8,128)(2,1)}, u32[]{:S(2)}) copy-start(bf16[1280,1280]{1,0:T(8,128)(2,1)} %param.16) | copy-start | bytes 9830404
  7.2 103.7 %all-gather.4.cloned.1.call-start = ((), (), s32[]{:S(2)}) async-start(), calls=%async_computation | async-start | bytes 4792320 | tf_op jit(solution)/shard_map/all_gather | solution.py:228
  10.3 2.0 collective-permute-start
  10.3 6.4 %copy-start.9 = (s32[512]{0:T(512)S(1)}, s32[512]{0:T(512)}, u32[]{:S(2)}) copy-start(s32[512]{0:T(512)} %param.11) | copy-start | bytes 6148
  13.6 0.7 copy-start.7
  13.6 1.6 copy-start.8
  15.2 17.1 %collective-permute-start.1 = (bf16[256,1280]{1,0:T(8,128)(2,1)}, bf16[256,1280]{1,0:T(8,128)(2,1)}, u32[]{:S(2)}, u32[]{:S(2)}) collective-permute-start(bf16[256,1280]{1,0:T(8,128)(2,1)} %pad_maximum_fusion), channel_id=1, source_target_pairs={{0,2},{1,3},{2,0},{3,1},{4,6},{5,7},{6,4},{7,5},{8,10},{9,11},{10,... | collective-permute-start | bytes 1966088 | tf_op jit(solution)/shard_map/ppermute | solution.py:31
  16.7 17.0 %copy-start.13 = (bf16[1280,4,192]{0,2,1:T(8,128)(2,1)S(1)}, bf16[1280,4,192]{0,2,1:T(8,128)(2,1)}, u32[]{:S(2)}) copy-start(bf16[1280,4,192]{0,2,1:T(8,128)(2,1)} %param.13) | copy-start | bytes 5898244
  36.2 1.9 copy-start.12
  156.7 2.2 collective-permute-start.2
  159.0 1.6 copy-start.10
  159.1 16.8 %collective-permute-start.3 = (f32[1,128,1280]{2,1,0:T(8,128)S(1)}, f32[1,128,1280]{2,1,0:T(8,128)S(1)}, u32[]{:S(2)}, u32[]{:S(2)}) collective-permute-start(f32[1,128,1280]{2,1,0:T(8,128)S(1)} %select_bitcast_fusion.2), channel_id=1, source_target_pairs={{0,2},{1,3},{2,0},{3,1},{4,6},{5,7},{6,4},{7,5},{8,10},{9,11},{10,... | collective-permute-start | bytes 1966088 | tf_op jit(solution)/shard_map/ppermute | solution.py:66
  160.7 15.5 %copy-start.3 = (bf16[128,1280]{1,0:T(8,128)(2,1)S(1)}, bf16[128,1280]{1,0:T(8,128)(2,1)}, u32[]{:S(2)}) copy-start(bf16[128,1280]{1,0:T(8,128)(2,1)} %param.10) | copy-start | bytes 983044
  176.2 2.4 %copy-start.1 = (f32[1,128,1280]{2,1,0:T(8,128)}, f32[1,128,1280]{2,1,0:T(8,128)S(1)}, u32[]{:S(2)}) copy-start(f32[1,128,1280]{2,1,0:T(8,128)S(1)} %get-tuple-element.9) | copy-start | bytes 1966084
  176.8 3.4 %copy-start.11 = (f32[2,1280]{1,0:T(2,128)S(1)}, f32[2,1280]{1,0:T(2,128)}, u32[]{:S(2)}) copy-start(f32[2,1280]{1,0:T(2,128)} %param.18) | copy-start | bytes 30724
  176.8 1.7 collective-permute-start.4
  178.6 16.8 %collective-permute-start.5 = (bf16[256,1280]{1,0:T(8,128)(2,1)S(1)}, bf16[256,1280]{1,0:T(8,128)(2,1)S(1)}, u32[]{:S(2)}, u32[]{:S(2)}) collective-permute-start(bf16[256,1280]{1,0:T(8,128)(2,1)S(1)} %pad_maximum_fusion.1), channel_id=1, source_target_pairs={{0,2},{1,3},{2,0},{3,1},{4,6},{5,7},{6,4},{7,5},{8,10},{9,11},{10,... | collective-permute-start | bytes 1966088 | tf_op jit(solution)/shard_map/ppermute | solution.py:31
  204.6 2.2 collective-permute-start.6
  207.0 1.1 copy-start.5
  208.1 2.4 %copy-start.14 = (s32[32]{0:T(128)S(1)}, s32[32]{0:T(128)}, u32[]{:S(2)}) copy-start(s32[32]{0:T(128)} %param.12) | copy-start | bytes 388
  209.0 17.1 %collective-permute-start.7 = (f32[1,128,1280]{2,1,0:T(8,128)}, f32[1,128,1280]{2,1,0:T(8,128)}, u32[]{:S(2)}, u32[]{:S(2)}) collective-permute-start(f32[1,128,1280]{2,1,0:T(8,128)} %select_bitcast_fusion), channel_id=1, source_target_pairs={{0,2},{1,3},{2,0},{3,1},{4,6},{5,7},{6,4},{7,5},{8,10},{9,11},{10,... | collective-permute-start | bytes 1966088 | tf_op jit(solution)/shard_map/ppermute | solution.py:66
  221.5 4.6 %copy-start.6 = (f32[1,2,128,1280]{3,2,1,0:T(8,128)S(1)}, f32[1,2,128,1280]{3,2,1,0:T(8,128)}, u32[]{:S(2)}) copy-start(f32[1,2,128,1280]{3,2,1,0:T(8,128)} %copy-done.5) | copy-start | bytes 3932164
  223.7 3.7 %copy-start.2 = (f32[1,128,1280]{2,1,0:T(8,128)S(1)}, f32[1,128,1280]{2,1,0:T(8,128)}, u32[]{:S(2)}) copy-start(f32[1,128,1280]{2,1,0:T(8,128)} %copy-done.1) | copy-start | bytes 1966084
  223.7 3.7 %copy-start.4 = (bf16[128,1280]{1,0:T(8,128)(2,1)S(1)}, bf16[128,1280]{1,0:T(8,128)(2,1)}, u32[]{:S(2)}) copy-start(bf16[128,1280]{1,0:T(8,128)(2,1)} %param.10) | copy-start | bytes 983044
Sparse Core Ops, SparseCore 0:
  37.4 73.4 all-gather.3
